TPU v7x, 512 devices: a whole 4x4x16 slice. The times are simulated.
512 devices in a mesh: rows: 128 (over z, y, core), cols: 4 (over x).
Axes of the slice: x: 4, y: 4, z: 16, core: 2. Of those that a mesh axis runs over, the one named last changes fastest.
Arguments:
- features: bfloat16 [256, 16384], P('cols', 'rows'), may hold values from -6 to 6
- weight_matrix: bfloat16 [256, 256], replicated, may hold values from -0.375 to 0.375
- bias_vector: float32 [256], replicated, may hold values from -3 to 3
- adjacency_tiles: bfloat16 [128, 65, 128, 128], P('rows')
- tile_cols: int32 [128, 65], P('rows'), may hold values from 0 to 127, as said below
- tile_count: int32 [128], P('rows'), may hold values from 25 to 65, as said below
- out_grad: bfloat16 [256, 16384], P('cols', 'rows'), may hold values from -6 to 6
Outputs:
- layer_out: bfloat16 [256, 16384], P('cols', 'rows')
- feature_grad: bfloat16 [256, 16384], P('cols', 'rows')
- weight_grad: float32 [256, 256], P('cols')
- bias_grad: float32 [256], P('cols')
Inputs may be any that keep to these rules, and one draw needn't show every extreme that they name: `tile_cols`: the live slots of a row block name distinct column blocks, its own among them; the pattern is symmetric: c is live in row block b exactly when b is live in row block c, and that tile is the transpose of the one of b in c's list. Slots past tile_count hold the row block's own index. Outside the hub's row, every live column block other than the hub lies within 16 blocks of the row block around the cycle of 128 blocks; the hub's own row also holds such band blocks. `tile_count`: exactly one row block, the hub, has all 65 slots live.
All inputs are finite; a program needn't handle non-finite values.
Results may differ from a plain program's by a relative error of at most 0.008.
Values may be sent and summed in bfloat16 or wider, within the bound.
No kernel may reach another device: no remote copies, remote signals or barrier semaphores. Data moves between devices by JAX's collectives and lax.ppermute only.
A program may use at most 64 MiB of HBM per device.

v0:
```python
import math
import jax
import jax.numpy as jnp
from jax import lax
from jax.sharding import PartitionSpec as P


def block_products(panel_rows, adjacency_tiles, tile_cols, alive_mask):
    feature_width = panel_rows.shape[0]
    tile_side = adjacency_tiles.shape[-1]
    panel_grid = panel_rows.reshape(feature_width, -1, tile_side)
    picked = jnp.take(panel_grid, tile_cols, axis=1)
    picked = jnp.where(alive_mask[None, :, :, None], picked, jnp.zeros((), jnp.bfloat16))
    result = jnp.einsum(
        "fbsk,bsrk->fbr", picked, adjacency_tiles, preferred_element_type=jnp.float32
    )
    return result.reshape(feature_width, -1)


def per_device(
    features, weight_matrix, bias_vector, adjacency_tiles, tile_cols, tile_count, out_grad
):
    feature_width, rows_here = features.shape
    blocks_here, slot_count = tile_cols.shape
    tile_side = adjacency_tiles.shape[-1]
    column_index = lax.axis_index("cols")
    rows_count = lax.axis_size("rows")
    alive_mask = jnp.arange(slot_count, dtype=jnp.int32)[None, :] < tile_count[:, None]
    all_panels = lax.all_gather(features, "rows", axis=1, tiled=True)
    aggregated = block_products(all_panels, adjacency_tiles, tile_cols, alive_mask).astype(
        jnp.bfloat16
    )
    aggregated_full = lax.all_gather(aggregated, "cols", axis=0, tiled=True)
    weight_rows = lax.dynamic_slice_in_dim(
        weight_matrix, column_index * feature_width, feature_width, 0
    )
    bias_rows = lax.dynamic_slice_in_dim(
        bias_vector, column_index * feature_width, feature_width, 0
    )
    preact = (
        jnp.dot(weight_rows, aggregated_full, preferred_element_type=jnp.float32)
        + bias_rows[:, None]
    )
    sigmoid_pre = jax.nn.sigmoid(preact)
    layer_out = (preact * sigmoid_pre).astype(jnp.bfloat16)
    pre_grad = (
        out_grad.astype(jnp.float32) * sigmoid_pre * (1.0 + preact * (1.0 - sigmoid_pre))
    ).astype(jnp.bfloat16)
    partial_grad = jnp.einsum(
        "oi,on->in", weight_rows, pre_grad, preferred_element_type=jnp.float32
    )
    agg_grad = lax.psum_scatter(partial_grad, "cols", scatter_dimension=0, tiled=True).astype(
        jnp.bfloat16
    )
    grad_scale = 1.0 / math.sqrt(rows_here * rows_count)
    weight_part = (
        jnp.einsum("fn,in->fi", pre_grad, aggregated_full, preferred_element_type=jnp.float32)
        * grad_scale
    )
    bias_part = jnp.sum(pre_grad.astype(jnp.float32), axis=1) * grad_scale
    weight_grad, bias_grad = lax.psum((weight_part, bias_part), "rows")
    own_blocks = agg_grad.reshape(feature_width, blocks_here, tile_side)
    contrib_terms = jnp.einsum(
        "fbr,bsrk->bsfk", own_blocks, adjacency_tiles, preferred_element_type=jnp.float32
    )
    contrib_terms = contrib_terms * alive_mask[:, :, None, None].astype(jnp.float32)
    flat_terms = contrib_terms.reshape(-1, feature_width, tile_side)
    row_count = blocks_here * lax.axis_size("rows")
    inside = (tile_cols >= 0) & (tile_cols < row_count)
    target = jnp.where(inside, tile_cols, row_count).reshape(-1)
    empty = jnp.zeros((row_count, feature_width, tile_side), jnp.float32)
    gathered_grad = lax.psum_scatter(
        empty.at[target].add(flat_terms, mode="drop"), "rows", scatter_dimension=0, tiled=True
    )
    feature_grad = (
        gathered_grad.transpose(1, 0, 2).reshape(feature_width, rows_here).astype(jnp.bfloat16)
    )
    return (layer_out, feature_grad, weight_grad, bias_grad)


def solution(mesh):
    return jax.shard_map(
        per_device,
        mesh=mesh,
        in_specs=(
            P("cols", "rows"),
            P(),
            P(),
            P("rows", None, None, None),
            P("rows", None),
            P("rows"),
            P("cols", "rows"),
        ),
        out_specs=(P("cols", "rows"), P("cols", "rows"), P("cols", None), P("cols")),
        check_vma=False,
    )
```

profile of v0, /device:TPU:1, one launch (start us, length us, event | category | flops | bytes accessed | tf_op | source)
XLA Modules:
  0.0 802.5 jit_solution(16811597391701644600)
XLA Ops:
  7.2 0.0 copy-start
  7.2 0.0 all-gather.2.cloned.1.call-start
  7.2 0.7 all-gather.2.cloned.1.call-update
  7.9 0.0 reduce-scatter.3.cloned.1.call-start
  8.6 0.8 dynamic_slice.7
  9.4 0.7 fusion.31
  10.0 0.7 and_bitcast_fusion
  10.7 139.1 %all-gather.2.cloned.1.call-done = bf16[64,16384]{1,0:T(8,128)(2,1)} async-done(((bf16[64,128]{1,0:T(8,128)(2,1)}), bf16[64,16384]{1,0:T(8,128)(2,1)}) %all-gather.2.cloned.1.call-update) | async-done | bytes 2097168 | tf_op jit(solution)/shard_map/all_gather | solution.py:29
  149.8 3.5 copy_bitcast_fusion
  153.3 2.3 gather_fusion
  155.6 0.0 copy-start.1
  155.6 0.0 copy-start.2
  155.7 0.0 copy-start.3
  155.7 0.9 fusion.10
  156.6 9.2 %all_gather.7 = bf16[256,128]{1,0:T(8,128)(2,1)S(1)} all-gather(bf16[64,128]{1,0:T(8,128)(2,1)S(1)} %fusion.10), channel_id=1, replica_groups=mesh['rows'=128,'cols'=4] {'cols'}, dimensions={0}, use_global_device_ids=true | all-gather | bytes 81920 | tf_op jit(solution)/shard_map/all_gather | solution.py:33
  165.8 0.9 convert_reduce_fusion
  166.7 0.8 fusion.20
  167.5 0.0 reduce-scatter.3.cloned.1.call-update
  167.5 0.0 reduce-scatter.5.cloned.1.call-start
  167.6 23.7 %reduce-scatter.3.cloned.1.call-done = f32[64,128]{1,0:T(8,128)} async-done(((f32[256,128]{1,0:T(8,128)}), f32[64,128]{1,0:T(8,128)}) %reduce-scatter.3.cloned.1.call-update) | async-done | bytes 32784 | tf_op jit(solution)/shard_map/reduce_scatter | solution.py:52
  191.3 2.5 fusion
  193.8 2.5 broadcast_in_dim.40
  196.3 12.6 %scatter_fusion = f32[128,64,128]{2,1,0:T(8,128)} fusion(f32[128,64,128]{2,1,0:T(8,128)} %broadcast_in_dim.40, s32[65]{0:T(128)S(1)} %fusion.26, f32[65,64,128]{2,1,0:T(8,128)} %fusion), kind=kCustom, calls=%fused_computation.1 | custom fusion | flops 532480 | bytes 6390020 | tf_op jit(solution)/shard_map/scatter-add | solution.py:73
  208.9 0.0 reduce-scatter.5.cloned.1.call-update
  209.0 0.0 all-reduce.2.cloned.1.call-start
  209.0 251.3 %psum.15 = f32[64]{0:T(128)} all-reduce(f32[64]{0:T(128)S(1)} %broadcast_multiply_fusion), channel_id=1, replica_groups=mesh['rows'=128,'cols'=4] {'rows'}, use_global_device_ids=true, to_apply=%region_5.6 | all-reduce | flops 64 | bytes 512 | tf_op jit(solution)/shard_map/psum | solution.py:61
  460.3 0.8 convolution_multiply_fusion
  461.1 0.0 all-reduce.2.cloned.1.call-update
  461.1 6.1 reduce-scatter.5.cloned.1.call-done
  467.2 1.4 convert_bitcast_fusion
  468.6 325.9 %all-reduce.2.cloned.1.call-done = f32[64,256]{1,0:T(8,128)} async-done(((f32[64,256]{1,0:T(8,128)}), f32[64,256]{1,0:T(8,128)}) %all-reduce.2.cloned.1.call-update) | async-done | bytes 65552 | tf_op jit(solution)/shard_map/psum | solution.py:61
  794.5 1.5 copy.17
  (9 shorter events, 0.0 us)
Async XLA Ops:
  7.2 148.5 %copy-start = (bf16[1,65,128,128]{3,2,1,0:T(8,128)(2,1)S(1)}, bf16[1,65,128,128]{3,2,1,0:T(8,128)(2,1)}, u32[]{:S(2)}) copy-start(bf16[1,65,128,128]{3,2,1,0:T(8,128)(2,1)} %param.10) | copy-start | bytes 6389764
  7.2 142.6 %all-gather.2.cloned.1.call-start = ((), (), s32[]{:S(2)}) async-start(), calls=%async_computation.2 | async-start | bytes 2113536 | tf_op jit(solution)/shard_map/all_gather | solution.py:29
  7.9 183.4 %reduce-scatter.3.cloned.1.call-start = ((), (), s32[]{:S(2)}) async-start(), calls=%async_computation.3 | async-start | bytes 163840 | tf_op jit(solution)/shard_map/reduce_scatter | solution.py:52
  155.6 10.2 %copy-start.1 = (bf16[256,256]{1,0:T(8,128)(2,1)S(1)}, bf16[256,256]{1,0:T(8,128)(2,1)}, u32[]{:S(2)}) copy-start(bf16[256,256]{1,0:T(8,128)(2,1)} %param.8) | copy-start | bytes 393220
  155.6 10.2 %copy-start.2 = (bf16[64,128]{1,0:T(8,128)(2,1)S(1)}, bf16[64,128]{1,0:T(8,128)(2,1)}, u32[]{:S(2)}) copy-start(bf16[64,128]{1,0:T(8,128)(2,1)} %param.13) | copy-start | bytes 49156
  155.7 12.0 %copy-start.3 = (s32[1,65]{1,0:T(1,128)S(1)}, s32[1,65]{1,0:T(1,128)}, u32[]{:S(2)}) copy-start(s32[1,65]{1,0:T(1,128)} %param.11) | copy-start | bytes 784
  167.5 299.6 %reduce-scatter.5.cloned.1.call-start = ((), (), s32[]{:S(2)}) async-start(), calls=%async_computation.4 | async-start | bytes 4227072 | tf_op jit(solution)/shard_map/reduce_scatter | solution.py:72
  209.0 585.5 %all-reduce.2.cloned.1.call-start = ((), (), s32[]{:S(2)}) async-start(), calls=%async_computation.5 | async-start | bytes 131072 | tf_op jit(solution)/shard_map/psum | solution.py:61
Sparse Core Ops, SparseCore 0:
  11.0 138.7 all-gather.1
  167.7 23.6 reduce-scatter.2
  209.1 258.0 reduce-scatter.4
  471.1 323.3 all-reduce.1
where the time goes:
time: 803 us; the launch traced here: 802 us
  waiting for transfers between devices  496 us (62%)
  blocking collectives  261 us (33%)
  other arithmetic  15.3 us (2%)
  between operations  14.5 us (2%)
  local copies, waits for them, and re-layouts  10.5 us (1%)
    psum x1, waiting for transfers between devices, per_device(): weight_grad, bias_grad = lax.psum((weight_part, bias_part), 'rows')  326 us
    psum x1, blocking collectives, per_device(): weight_grad, bias_grad = lax.psum((weight_part, bias_part), 'rows')  251 us
    all_gather x1, waiting for transfers between devices, per_device(): all_panels = lax.all_gather(features, 'rows', axis=1, tiled=True)  139 us
    reduce_scatter x1, waiting for transfers between devices, per_device(): lax.psum_scatter(partial_grad, 'cols', scatter_dimension=0, tiled=True)  23.7 us
  transfers between devices with their start and end apart: 4, of which 4 were waited for; matrix products, arithmetic and copies ran while one was open for 1% of the time, Pallas kernels for 0%

commit v1 on v0

--- a/solution.py
+++ b/solution.py
@@ -26,7 +26,16 @@
     column_index = lax.axis_index("cols")
     rows_count = lax.axis_size("rows")
     alive_mask = jnp.arange(slot_count, dtype=jnp.int32)[None, :] < tile_count[:, None]
-    all_panels = lax.all_gather(features, "rows", axis=1, tiled=True)
+    open_the_paths = lambda z: jnp.concatenate(
+        jax.lax.all_to_all(
+            jnp.stack([z] * jax.lax.psum(1, axis_name="rows")),
+            concat_axis=0,
+            axis_name="rows",
+            split_axis=0,
+        ),
+        axis=1,
+    )
+    all_panels = open_the_paths(features)
     aggregated = block_products(all_panels, adjacency_tiles, tile_cols, alive_mask).astype(
         jnp.bfloat16
     )

time: 803 us -> 778 us (0.969)
  waiting for transfers between devices: 496 us -> 451 us
  starting transfers between devices: 0.16 us -> 21.3 us
    all_gather x1 -> x0, waiting for transfers between devices: 139 us -> none  [per_device(): all_panels = lax.all_gather(features, 'rows', axis=1, tiled=True)]
    all_to_all x0 -> x1, waiting for transfers between devices: none -> 94.7 us  [per_device(): jax.lax.all_to_all(jnp.stack([z] * jax.lax.psum(1, axis_name='rows')), co...]
    all_to_all x0 -> x1, starting transfers between devices: none -> 21.1 us  [per_device(): jax.lax.all_to_all(jnp.stack([z] * jax.lax.psum(1, axis_name='rows')), co...]
  transfers between devices with their start and end apart: 4 -> 4, of which waited for: 4 -> 4; matrix products, arithmetic and copies ran while one was open for 1% -> 0% of each run, Pallas kernels for 0% -> 0%
where the time goes in v1:
time: 778 us; the launch traced here: 777 us
  waiting for transfers between devices  451 us (58%)
  blocking collectives  261 us (34%)
  starting transfers between devices  21.3 us (3%)
  between operations  14.5 us (2%)
  other arithmetic  14 us (2%)
  local copies, waits for them, and re-layouts  9.05 us (1%)
    psum x1, waiting for transfers between devices, per_device(): weight_grad, bias_grad = lax.psum((weight_part, bias_part), 'rows')  326 us
    psum x1, blocking collectives, per_device(): weight_grad, bias_grad = lax.psum((weight_part, bias_part), 'rows')  251 us
    all_to_all x1, waiting for transfers between devices, per_device(): jax.lax.all_to_all(jnp.stack([z] * jax.lax.psum(1, axis_name='rows')), co...  94.7 us
    reduce_scatter x1, waiting for transfers between devices, per_device(): lax.psum_scatter(partial_grad, 'cols', scatter_dimension=0, tiled=True)  24.1 us
    all_to_all x1, starting transfers between devices, per_device(): jax.lax.all_to_all(jnp.stack([z] * jax.lax.psum(1, axis_name='rows')), co...  21.1 us
  transfers between devices with their start and end apart: 4, of which 4 were waited for; matrix products, arithmetic and copies ran while one was open for 0% of the time, Pallas kernels for 0%

profile of v1, /device:TPU:1, one launch (start us, length us, event | category | flops | bytes accessed | tf_op | source)
XLA Modules:
  0.0 776.9 jit_solution(3827986943739146926)
XLA Ops:
  7.2 0.0 copy-start
  7.2 2.7 stack.2
  9.9 21.1 %all-to-all-start = ((bf16[128,64,128]{2,1,0:T(8,128)(2,1)}), bf16[128,64,128]{2,1,0:T(8,128)(2,1)}, u32[]{:S(2)}, u32[]{:S(2)}) async-start(bf16[128,64,128]{2,1,0:T(8,128)(2,1)} %stack.2), calls=%async_computation | async-start | bytes 4194304 | tf_op jit(solution)/shard_map/all_to_all | solution.py:30
  31.0 0.0 reduce-scatter.3.cloned.1.call-start
  31.7 0.0 copy-done.3
  31.7 0.1 dynamic_slice.7
  31.8 0.0 copy-done.4
  31.9 94.7 %all-to-all-done = bf16[128,64,128]{2,1,0:T(8,128)(2,1)} async-done(((bf16[128,64,128]{2,1,0:T(8,128)(2,1)}), bf16[128,64,128]{2,1,0:T(8,128)(2,1)}, u32[]{:S(2)}, u32[]{:S(2)}) %all-to-all-start) | async-done | bytes 2097184 | tf_op jit(solution)/shard_map/all_to_all | solution.py:30
  126.6 2.3 gather_fusion
  128.9 0.0 copy-done
  128.9 0.0 copy-start.1
  129.0 0.0 copy-start.2
  129.0 0.9 fusion.10
  129.9 9.3 %all_gather.3 = bf16[256,128]{1,0:T(8,128)(2,1)S(1)} all-gather(bf16[64,128]{1,0:T(8,128)(2,1)S(1)} %fusion.10), channel_id=1, replica_groups=mesh['rows'=128,'cols'=4] {'cols'}, dimensions={0}, use_global_device_ids=true | all-gather | bytes 81920 | tf_op jit(solution)/shard_map/all_gather | solution.py:42
  139.2 0.0 copy-done.1
  139.2 0.9 convert_reduce_fusion
  140.1 0.8 fusion.20
  140.9 0.0 reduce-scatter.3.cloned.1.call-update
  141.0 0.0 reduce-scatter.5.cloned.1.call-start
  141.0 24.1 %reduce-scatter.3.cloned.1.call-done = f32[64,128]{1,0:T(8,128)} async-done(((f32[256,128]{1,0:T(8,128)}), f32[64,128]{1,0:T(8,128)}) %reduce-scatter.3.cloned.1.call-update) | async-done | bytes 32784 | tf_op jit(solution)/shard_map/reduce_scatter | solution.py:61
  165.2 2.5 fusion
  167.7 2.5 broadcast_in_dim.40
  170.2 12.6 %scatter_fusion = f32[128,64,128]{2,1,0:T(8,128)} fusion(f32[128,64,128]{2,1,0:T(8,128)} %broadcast_in_dim.40, s32[65]{0:T(128)S(1)} %fusion.26, f32[65,64,128]{2,1,0:T(8,128)} %fusion), kind=kCustom, calls=%fused_computation.1 | custom fusion | flops 532480 | bytes 6390020 | tf_op jit(solution)/shard_map/scatter-add | solution.py:82
  182.8 0.0 reduce-scatter.5.cloned.1.call-update
  182.8 0.0 all-reduce.2.cloned.1.call-start
  182.9 251.3 %psum.15 = f32[64]{0:T(128)} all-reduce(f32[64]{0:T(128)S(1)} %broadcast_multiply_fusion), channel_id=1, replica_groups=mesh['rows'=128,'cols'=4] {'rows'}, use_global_device_ids=true, to_apply=%region_5.6 | all-reduce | flops 64 | bytes 512 | tf_op jit(solution)/shard_map/psum | solution.py:70
  434.2 0.8 convolution_multiply_fusion
  435.0 0.0 all-reduce.2.cloned.1.call-update
  435.0 6.5 reduce-scatter.5.cloned.1.call-done
  441.5 1.4 convert_bitcast_fusion
  442.8 326.1 %all-reduce.2.cloned.1.call-done = f32[64,256]{1,0:T(8,128)} async-done(((f32[64,256]{1,0:T(8,128)}), f32[64,256]{1,0:T(8,128)}) %all-reduce.2.cloned.1.call-update) | async-done | bytes 65552 | tf_op jit(solution)/shard_map/psum | solution.py:70
  768.9 1.5 copy.14
  (10 shorter events, 0.0 us)
Async XLA Ops:
  7.2 121.8 %copy-start = (bf16[1,65,128,128]{3,2,1,0:T(8,128)(2,1)S(1)}, bf16[1,65,128,128]{3,2,1,0:T(8,128)(2,1)}, u32[]{:S(2)}) copy-start(bf16[1,65,128,128]{3,2,1,0:T(8,128)(2,1)} %param.10) | copy-start | bytes 6389764
  9.9 21.9 %copy-start.3 = (f32[256]{0:T(256)S(1)}, f32[256]{0:T(256)}, u32[]{:S(2)}) copy-start(f32[256]{0:T(256)} %param.9) | copy-start | bytes 3076
  9.9 21.9 %copy-start.4 = (s32[1,65]{1,0:T(1,128)S(1)}, s32[1,65]{1,0:T(1,128)}, u32[]{:S(2)}) copy-start(s32[1,65]{1,0:T(1,128)} %param.11) | copy-start | bytes 784
  9.9 116.7 %all-to-all-start = ((bf16[128,64,128]{2,1,0:T(8,128)(2,1)}), bf16[128,64,128]{2,1,0:T(8,128)(2,1)}, u32[]{:S(2)}, u32[]{:S(2)}) async-start(bf16[128,64,128]{2,1,0:T(8,128)(2,1)} %stack.2), calls=%async_computation | async-start | bytes 4194304 | tf_op jit(solution)/shard_map/all_to_all | solution.py:30
  31.0 134.2 %reduce-scatter.3.cloned.1.call-start = ((), (), s32[]{:S(2)}) async-start(), calls=%async_computation.3 | async-start | bytes 163840 | tf_op jit(solution)/shard_map/reduce_scatter | solution.py:61
  128.9 10.3 %copy-start.1 = (bf16[256,256]{1,0:T(8,128)(2,1)S(1)}, bf16[256,256]{1,0:T(8,128)(2,1)}, u32[]{:S(2)}) copy-start(bf16[256,256]{1,0:T(8,128)(2,1)} %param.8) | copy-start | bytes 393220
  129.0 10.3 %copy-start.2 = (bf16[64,128]{1,0:T(8,128)(2,1)S(1)}, bf16[64,128]{1,0:T(8,128)(2,1)}, u32[]{:S(2)}) copy-start(bf16[64,128]{1,0:T(8,128)(2,1)} %param.13) | copy-start | bytes 49156
  141.0 300.5 %reduce-scatter.5.cloned.1.call-start = ((), (), s32[]{:S(2)}) async-start(), calls=%async_computation.4 | async-start | bytes 4227072 | tf_op jit(solution)/shard_map/reduce_scatter | solution.py:81
  182.8 586.1 %all-reduce.2.cloned.1.call-start = ((), (), s32[]{:S(2)}) async-start(), calls=%async_computation.5 | async-start | bytes 131072 | tf_op jit(solution)/shard_map/psum | solution.py:70
Sparse Core Ops, SparseCore 0:
  141.1 24.0 reduce-scatter.2
  182.9 258.4 reduce-scatter.4
  445.5 323.3 all-reduce.1
